TPU v7x, 256 devices: a whole 4x4x8 slice. The times are simulated.
256 devices in a mesh: dp: 16 (over z_lo, x), tensor: 16 (over z_hi, y, core).
Axes of the slice: x: 4, y: 4, z: 8 (z_hi: 2, z_lo: 4; z = z_hi * 4 + z_lo), core: 2. Of those that a mesh axis runs over, the one named last changes fastest.
Arguments:
- cotangent: bfloat16 [8192, 4096], P(('dp', 'tensor')), may hold values from -6 to 6
- gate: bfloat16 [8192, 14336], P('dp', 'tensor'), may hold values from -8 to 8
- up: bfloat16 [8192, 14336], P('dp', 'tensor'), may hold values from -6 to 6
- w_down: bfloat16 [4, 14336, 4096], P(None, 'tensor', 'dp'), may hold values from -0.03125 to 0.03125
- language: int32 [16], replicated, may hold values from 0 to 3
Outputs:
- d_gate: bfloat16 [8192, 14336], P('dp', 'tensor')
- d_up: bfloat16 [8192, 14336], P('dp', 'tensor')
- d_weight: float32 [4, 14336, 4096], P(None, 'tensor', 'dp')
All inputs are finite; a program needn't handle non-finite values.
Results may differ from a plain program's by a relative error of at most 0.0029.
Values may be sent and summed in bfloat16 or wider, within the bound.
No kernel may reach another device: no remote copies, remote signals or barrier semaphores. Data moves between devices by JAX's collectives and lax.ppermute only.
A program may use at most 128 MiB of HBM per device.

v0:
```python
import jax
import jax.numpy as jnp
from jax import lax
from jax.sharding import PartitionSpec as P


def shards(cotangent, gate, up, w_down, language):
    groups = lax.axis_size("dp")
    variants = w_down.shape[0]
    ff_dev = w_down.shape[1]
    feat_dev = w_down.shape[2]
    out_rows = lax.all_gather(cotangent, "tensor", axis=0, tiled=True)
    gate_f = gate.astype(jnp.float32)
    up_f = up.astype(jnp.float32)
    sig = jax.nn.sigmoid(gate_f)
    act = gate_f * sig
    hidden = (act * up_f).astype(jnp.bfloat16)
    slabs = jnp.take(w_down, language, axis=0)
    received = lax.all_to_all(slabs, "dp", split_axis=0, concat_axis=2, tiled=True)
    weights = received[0]
    d_hidden = lax.dot_general(
        out_rows, weights, (((1,), (1,)), ((), ())), preferred_element_type=jnp.float32
    )
    d_up = (d_hidden * act).astype(jnp.bfloat16)
    d_gate = (d_hidden * up_f * sig * (1.0 + gate_f * (1.0 - sig))).astype(jnp.bfloat16)
    selector = (language[None, :] == jnp.arange(variants, dtype=jnp.int32)[:, None]).astype(
        jnp.float32
    )
    partial_term = lax.dot_general(
        hidden, out_rows, (((0,), (0,)), ((), ())), preferred_element_type=jnp.float32
    )
    pieces = lax.all_to_all(
        partial_term.reshape(ff_dev, groups, feat_dev),
        "dp",
        split_axis=1,
        concat_axis=1,
        tiled=True,
    )
    d_weight = jnp.einsum("lg,fgd->lfd", selector, pieces, precision=lax.Precision.HIGHEST)
    return (d_gate, d_up, d_weight)


def solution(mesh):
    return jax.shard_map(
        shards,
        mesh=mesh,
        in_specs=(
            P(("dp", "tensor"), None),
            P("dp", "tensor"),
            P("dp", "tensor"),
            P(None, "tensor", "dp"),
            P(),
        ),
        out_specs=(P("dp", "tensor"), P("dp", "tensor"), P(None, "tensor", "dp")),
        check_vma=False,
    )
```

profile of v0, /device:TPU:64, one launch (start us, length us, event | category | flops | bytes accessed | tf_op | source)
XLA Modules:
  0.0 566.6 jit_solution(13106661074899269644)
XLA Ops:
  7.2 0.0 copy-start
  7.2 0.8 compare_and_fusion
  8.0 0.7 compare_select_fusion
  8.6 0.0 copy-done
  8.7 4.0 gather_fusion
  12.7 6.9 %broadcast_select_fusion = bf16[16,896,256]{2,1,0:T(8,128)(2,1)} fusion(bf16[16,896,256]{2,1,0:T(8,128)(2,1)} %gather_fusion, pred[16]{0:T(512)(128)(4,1)S(1)} %compare_and_fusion), kind=kLoop, calls=%fused_computation.4 | loop fusion | flops 3670016 | bytes 14680080 | tf_op jit(solution)/shard_map/jit(_take)/select_n | solution.py:18
  19.6 0.0 copy-start.2
  19.6 0.0 copy-start.3
  19.6 8.2 %all-to-all-start = ((bf16[16,896,256]{2,1,0:T(8,128)(2,1)}), bf16[16,896,256]{2,1,0:T(8,128)(2,1)}, u32[]{:S(2)}, u32[]{:S(2)}) async-start(bf16[16,896,256]{2,1,0:T(8,128)(2,1)} %broadcast_select_fusion), calls=%async_computation | async-start | bytes 14680064 | tf_op jit(solution)/shard_map/all_to_all | solution.py:19
  27.7 0.0 all-gather.2.cloned.1.call-start
  27.8 0.7 all-gather.2.cloned.1.call-update
  28.5 0.0 copy-done.2
  28.5 0.5 copy.26
  29.0 0.0 copy-done.3
  29.0 0.5 copy.25
  29.6 121.4 %all-gather.2.cloned.1.call-done = bf16[512,4096]{1,0:T(8,128)(2,1)} async-done(((bf16[32,4096]{1,0:T(8,128)(2,1)}), bf16[512,4096]{1,0:T(8,128)(2,1)}) %all-gather.2.cloned.1.call-update) | async-done | bytes 4194320 | tf_op jit(solution)/shard_map/all_gather | solution.py:12
  150.9 9.5 %fusion.11 = f32[896,4096]{1,0:T(8,128)} fusion(bf16[512,4096]{1,0:T(8,128)(2,1)} %all-gather.2.cloned.1.call-done, bf16[512,896]{0,1:T(8,128)(2,1)S(1)} %copy.25, bf16[512,896]{0,1:T(8,128)(2,1)S(1)} %copy.26), kind=kOutput, calls=%fused_computation.20 | convolution fusion | flops 3761766400 | bytes 20709376 | tf_op jit(solution)/shard_map/dot_general | solution.py:29
  160.4 12.0 %copy.36 = f32[112,16,8,256]{3,2,0,1:T(8,128)} copy(f32[112,16,8,256]{3,2,1,0:T(8,128)} %bitcast.20) | data formatting | bytes 29360128 | tf_op jit(solution)/shard_map/reshape | solution.py:33
  172.4 44.2 %all-to-all-done = bf16[16,896,256]{2,1,0:T(8,128)(2,1)} async-done(((bf16[16,896,256]{2,1,0:T(8,128)(2,1)}), bf16[16,896,256]{2,1,0:T(8,128)(2,1)}, u32[]{:S(2)}, u32[]{:S(2)}) %all-to-all-start) | async-done | bytes 7340064 | tf_op jit(solution)/shard_map/all_to_all | solution.py:19
  216.6 5.2 all-to-all-start.1
  221.7 11.1 %copy.24 = bf16[1,896,16,256]{1,3,2,0:T(8,128)(2,1)} copy(bf16[1,896,16,256]{3,1,2,0:T(8,128)(2,1)} %bitcast.1) | data formatting | bytes 14680064 | tf_op jit(solution)/shard_map/all_to_all | solution.py:19
  232.9 9.8 %fusion.10 = (bf16[512,896]{0,1:T(8,128)(2,1)}, bf16[512,896]{0,1:T(8,128)(2,1)S(1)}) fusion(bf16[512,896]{0,1:T(8,128)(2,1)S(1)} %copy.26, bf16[512,896]{0,1:T(8,128)(2,1)S(1)} %copy.25, bf16[896,4096]{0,1:T(8,128)(2,1)} %bitcast.21, bf16[512,4096]{1,0:T(8,128)(2,1)} %all-gather.2.cloned.1.call-done), kind=kOutput, calls=%fused_computation.19 | convolution fusion | flops 3764977664 | bytes 15204352 | tf_op jit(solution)/shard_map/dot_general | solution.py:21
  242.7 0.0 copy-start.4
  242.7 2.2 copy.30
  244.9 1.3 copy.29
  246.2 292.8 %all-to-all-done.1 = f32[896,16,256]{2,0,1:T(8,128)} async-done(((f32[896,16,256]{2,0,1:T(8,128)}), f32[896,16,256]{2,0,1:T(8,128)}, u32[]{:S(2)}, u32[]{:S(2)}) %all-to-all-start.1) | async-done | bytes 14680096 | tf_op jit(solution)/shard_map/all_to_all | solution.py:32
  539.0 0.0 copy-done.4
  539.0 0.0 copy-start.1
  539.0 18.3 %fusion = f32[4,896,256]{2,0,1:T(4,128)S(1)} fusion(f32[896,16,256]{2,0,1:T(8,128)} %all-to-all-done.1, s32[16]{0:T(128)S(1)} %copy-done.4), kind=kOutput, calls=%fused_computation.2 | convolution fusion | flops 176160832 | bytes 18350144 | tf_op jit(solution)/shard_map/lg,fgd->lfd/dot_general | solution.py:39
  557.3 2.5 copy.31
  559.8 0.0 copy-done.1
  (1 shorter events, 0.0 us)
Async XLA Ops:
  7.2 1.5 copy-start
  19.6 8.9 %copy-start.2 = (bf16[512,896]{1,0:T(8,128)(2,1)S(1)}, bf16[512,896]{1,0:T(8,128)(2,1)}, u32[]{:S(2)}) copy-start(bf16[512,896]{1,0:T(8,128)(2,1)} %param.6) | copy-start | bytes 2752516
  19.6 9.4 %copy-start.3 = (bf16[512,896]{1,0:T(8,128)(2,1)S(1)}, bf16[512,896]{1,0:T(8,128)(2,1)}, u32[]{:S(2)}) copy-start(bf16[512,896]{1,0:T(8,128)(2,1)} %param.7) | copy-start | bytes 2752516
  19.6 197.0 %all-to-all-start = ((bf16[16,896,256]{2,1,0:T(8,128)(2,1)}), bf16[16,896,256]{2,1,0:T(8,128)(2,1)}, u32[]{:S(2)}, u32[]{:S(2)}) async-start(bf16[16,896,256]{2,1,0:T(8,128)(2,1)} %broadcast_select_fusion), calls=%async_computation | async-start | bytes 14680064 | tf_op jit(solution)/shard_map/all_to_all | solution.py:19
  27.7 123.2 %all-gather.2.cloned.1.call-start = ((), (), s32[]{:S(2)}) async-start(), calls=%async_computation.2 | async-start | bytes 4456448 | tf_op jit(solution)/shard_map/all_gather | solution.py:12
  216.6 322.4 %all-to-all-start.1 = ((f32[896,16,256]{2,0,1:T(8,128)}), f32[896,16,256]{2,0,1:T(8,128)}, u32[]{:S(2)}, u32[]{:S(2)}) async-start(f32[896,16,256]{2,0,1:T(8,128)} %bitcast.19), calls=%async_computation.1 | async-start | bytes 29360128 | tf_op jit(solution)/shard_map/all_to_all | solution.py:32
  242.7 296.3 %copy-start.4 = (s32[16]{0:T(128)S(1)}, s32[16]{0:T(128)}, u32[]{:S(2)}) copy-start(s32[16]{0:T(128)} %param.9) | copy-start | bytes 196
  539.0 20.8 %copy-start.1 = (bf16[4,896,256]{2,1,0:T(8,128)(2,1)S(1)}, bf16[4,896,256]{2,1,0:T(8,128)(2,1)}, u32[]{:S(2)}) copy-start(bf16[4,896,256]{2,1,0:T(8,128)(2,1)} %param.8) | copy-start | bytes 5505028
Sparse Core Ops, SparseCore 0:
  31.3 119.5 all-gather.1
where the time goes:
time: 567 us
  waiting for transfers between devices  459 us (81%)
  matrix products  37.6 us (7%)
  local copies, waits for them, and re-layouts  34.2 us (6%)
  between operations  14.1 us (2%)
  starting transfers between devices  13.4 us (2%)
  other arithmetic  8.33 us (1%)
    all_to_all x1, waiting for transfers between devices, shards(): lax.all_to_all(partial_term.reshape(ff_dev, groups, feat_dev), 'dp', spli...  293 us
    all_gather x1, waiting for transfers between devices, shards(): out_rows = lax.all_gather(cotangent, 'tensor', axis=0, tiled=True)  121 us
    all_to_all x1, waiting for transfers between devices, shards(): lax.all_to_all(slabs, 'dp', split_axis=0, concat_axis=2, tiled=True)  44.2 us
    dot_general x1, matrix products, shards(): jnp.einsum('lg,fgd->lfd', selector, pieces, precision=lax.Precision.HIGHEST)  18.3 us
    reshape x1, local copies, waits for them, and re-layouts, shards(): partial_term.reshape(ff_dev, groups, feat_dev)  12 us
  transfers between devices with their start and end apart: 3, of which 3 were waited for; matrix products, arithmetic and copies ran while one was open for 8% of the time, Pallas kernels for 0%

commit v1 on v0

--- a/solution.py
+++ b/solution.py
@@ -9,7 +9,9 @@
     variants = w_down.shape[0]
     ff_dev = w_down.shape[1]
     feat_dev = w_down.shape[2]
-    out_rows = lax.all_gather(cotangent, "tensor", axis=0, tiled=True)
+    out_rows = jnp.concatenate(
+        lax.all_to_all(jnp.stack([cotangent] * lax.axis_size("tensor")), "tensor", 0, 0), axis=0
+    )
     gate_f = gate.astype(jnp.float32)
     up_f = up.astype(jnp.float32)
     sig = jax.nn.sigmoid(gate_f)

time: 567 us -> 631 us (1.11); the launches traced: 567 us -> 623 us
  waiting for transfers between devices: 459 us -> 524 us
  between operations: 14.1 us -> 0.72 us
  starting transfers between devices: 13.4 us -> 21.4 us
    all_gather x1 -> x0, waiting for transfers between devices: 121 us -> none  [shards(): out_rows = lax.all_gather(cotangent, 'tensor', axis=0, tiled=True)]
    all_to_all x1, waiting for transfers between devices: 44.2 us -> 143 us  [shards(): lax.all_to_all(slabs, 'dp', split_axis=0, concat_axis=2, tiled=True)]
    all_to_all x0 -> x1, waiting for transfers between devices: none -> 88.4 us  [shards(): lax.all_to_all(jnp.stack([cotangent] * lax.axis_size('tensor')), 'tensor'...]
    reshape x1 -> x0, local copies, waits for them, and re-layouts: 12 us -> none  [shards(): partial_term.reshape(ff_dev, groups, feat_dev)]
    all_to_all x0 -> x1, starting transfers between devices: none -> 9.58 us  [shards(): lax.all_to_all(jnp.stack([cotangent] * lax.axis_size('tensor')), 'tensor'...]
    dot_general x0 -> x1, local copies, waits for them, and re-layouts: none -> 6.62 us  [shards(): lax.dot_general(hidden, out_rows, (((0,), (0,)), ((), ())), preferred_ele...]
where the time goes in v1:
time: 631 us; the launch traced here: 623 us
  waiting for transfers between devices  524 us (83%)
  matrix products  37.6 us (6%)
  local copies, waits for them, and re-layouts  32.3 us (5%)
  starting transfers between devices  21.4 us (3%)
  other arithmetic  6.79 us (1%)
    all_to_all x1, waiting for transfers between devices, shards(): lax.all_to_all(partial_term.reshape(ff_dev, groups, feat_dev), 'dp', spli...  293 us
    all_to_all x1, waiting for transfers between devices, shards(): lax.all_to_all(slabs, 'dp', split_axis=0, concat_axis=2, tiled=True)  143 us
    all_to_all x1, waiting for transfers between devices, shards(): lax.all_to_all(jnp.stack([cotangent] * lax.axis_size('tensor')), 'tensor'...  88.4 us
    dot_general x1, matrix products, shards(): jnp.einsum('lg,fgd->lfd', selector, pieces, precision=lax.Precision.HIGHEST)  18.3 us
  transfers between devices with their start and end apart: 3, of which 3 were waited for; matrix products, arithmetic and copies ran while one was open for 8% of the time, Pallas kernels for 0%

profile of v1, /device:TPU:64, one launch (start us, length us, event | category | flops | bytes accessed | tf_op | source)
XLA Modules:
  0.0 623.3 jit_solution(1740007196001290812)
XLA Ops:
  0.6 0.0 copy-start
  0.6 3.5 stack.2
  4.2 0.0 copy-start.4
  4.2 9.6 %all-to-all-start.1 = ((bf16[16,32,4096]{2,1,0:T(8,128)(2,1)}), bf16[16,32,4096]{2,1,0:T(8,128)(2,1)}, u32[]{:S(2)}, u32[]{:S(2)}) async-start(bf16[16,32,4096]{2,1,0:T(8,128)(2,1)} %stack.2), calls=%async_computation.1 | async-start | bytes 8388608 | tf_op jit(solution)/shard_map/all_to_all | solution.py:13
  13.8 0.0 copy-done.4
  13.8 0.0 copy-done
  13.8 3.9 gather_fusion
  17.8 6.8 %broadcast_select_fusion = bf16[16,896,256]{2,1,0:T(8,128)(2,1)} fusion(bf16[16,896,256]{2,1,0:T(8,128)(2,1)} %gather_fusion, pred[16]{0:T(512)(128)(4,1)S(1)} %compare_and_fusion), kind=kLoop, calls=%fused_computation.3 | loop fusion | flops 3670016 | bytes 14680080 | tf_op jit(solution)/shard_map/jit(_take)/select_n | solution.py:20
  24.5 0.0 copy-start.2
  24.5 0.0 copy-start.3
  24.6 88.4 %all-to-all-done.1 = bf16[16,32,4096]{2,1,0:T(8,128)(2,1)} async-done(((bf16[16,32,4096]{2,1,0:T(8,128)(2,1)}), bf16[16,32,4096]{2,1,0:T(8,128)(2,1)}, u32[]{:S(2)}, u32[]{:S(2)}) %all-to-all-start.1) | async-done | bytes 4194336 | tf_op jit(solution)/shard_map/all_to_all | solution.py:13
  113.0 6.7 %all-to-all-start = ((bf16[16,896,256]{2,1,0:T(8,128)(2,1)}), bf16[16,896,256]{2,1,0:T(8,128)(2,1)}, u32[]{:S(2)}, u32[]{:S(2)}) async-start(bf16[16,896,256]{2,1,0:T(8,128)(2,1)} %broadcast_select_fusion), calls=%async_computation | async-start | bytes 14680064 | tf_op jit(solution)/shard_map/all_to_all | solution.py:21
  119.6 0.0 copy-done.2
  119.6 0.5 copy.28
  120.2 0.0 copy-done.3
  120.2 0.5 copy.27
  120.7 6.6 %copy.29 = bf16[4096,512]{1,0:T(8,128)(2,1)} copy(bf16[4096,512]{0,1:T(8,128)(2,1)} %bitcast.7) | data formatting | bytes 8388608 | tf_op jit(solution)/shard_map/dot_general | solution.py:31
  127.3 9.5 %fusion.12 = f32[896,16,256]{2,0,1:T(8,128)} fusion(bf16[16,256,512]{2,1,0:T(8,128)(2,1)} %bitcast.23, bf16[512,896]{0,1:T(8,128)(2,1)S(1)} %copy.27, bf16[512,896]{0,1:T(8,128)(2,1)S(1)} %copy.28), kind=kOutput, calls=%fused_computation.20 | convolution fusion | flops 3761766400 | bytes 20709376 | tf_op jit(solution)/shard_map/dot_general | solution.py:31
  136.8 143.3 %all-to-all-done = bf16[16,896,256]{2,1,0:T(8,128)(2,1)} async-done(((bf16[16,896,256]{2,1,0:T(8,128)(2,1)}), bf16[16,896,256]{2,1,0:T(8,128)(2,1)}, u32[]{:S(2)}, u32[]{:S(2)}) %all-to-all-start) | async-done | bytes 7340064 | tf_op jit(solution)/shard_map/all_to_all | solution.py:21
  280.1 5.2 all-to-all-start.2
  285.3 11.2 %copy.26 = bf16[1,896,16,256]{1,3,2,0:T(8,128)(2,1)} copy(bf16[1,896,16,256]{3,1,2,0:T(8,128)(2,1)} %bitcast.1) | data formatting | bytes 14680064 | tf_op jit(solution)/shard_map/all_to_all | solution.py:21
  296.4 9.8 %fusion.10 = (bf16[512,896]{0,1:T(8,128)(2,1)}, bf16[512,896]{0,1:T(8,128)(2,1)S(1)}) fusion(bf16[512,896]{0,1:T(8,128)(2,1)S(1)} %copy.28, bf16[512,896]{0,1:T(8,128)(2,1)S(1)} %copy.27, bf16[896,4096]{0,1:T(8,128)(2,1)} %bitcast.22, bf16[512,4096]{1,0:T(8,128)(2,1)} %bitcast.3), kind=kOutput, calls=%fused_computation.18 | convolution fusion | flops 3764977664 | bytes 15204352 | tf_op jit(solution)/shard_map/dot_general | solution.py:23
  306.3 2.2 copy.32
  308.5 1.3 copy.31
  309.7 292.8 %all-to-all-done.2 = f32[896,16,256]{2,0,1:T(8,128)} async-done(((f32[896,16,256]{2,0,1:T(8,128)}), f32[896,16,256]{2,0,1:T(8,128)}, u32[]{:S(2)}, u32[]{:S(2)}) %all-to-all-start.2) | async-done | bytes 14680096 | tf_op jit(solution)/shard_map/all_to_all | solution.py:34
  602.5 0.0 copy-start.1
  602.5 18.3 %fusion = f32[4,896,256]{2,0,1:T(4,128)S(1)} fusion(f32[896,16,256]{2,0,1:T(8,128)} %all-to-all-done.2, s32[16]{0:T(128)S(1)} %copy-done.4), kind=kOutput, calls=%fused_computation.1 | convolution fusion | flops 176160832 | bytes 18350144 | tf_op jit(solution)/shard_map/lg,fgd->lfd/dot_general | solution.py:41
  620.8 2.5 copy.33
  623.3 0.0 copy-done.1
  (3 shorter events, 0.0 us)
Async XLA Ops:
  0.6 13.2 %copy-start = (bf16[4,896,256]{2,1,0:T(8,128)(2,1)S(1)}, bf16[4,896,256]{2,1,0:T(8,128)(2,1)}, u32[]{:S(2)}) copy-start(bf16[4,896,256]{2,1,0:T(8,128)(2,1)} %param.8) | copy-start | bytes 5505028
  4.2 9.6 %copy-start.4 = (s32[16]{0:T(128)S(1)}, s32[16]{0:T(128)}, u32[]{:S(2)}) copy-start(s32[16]{0:T(128)} %param.9) | copy-start | bytes 196
  4.2 108.8 %all-to-all-start.1 = ((bf16[16,32,4096]{2,1,0:T(8,128)(2,1)}), bf16[16,32,4096]{2,1,0:T(8,128)(2,1)}, u32[]{:S(2)}, u32[]{:S(2)}) async-start(bf16[16,32,4096]{2,1,0:T(8,128)(2,1)} %stack.2), calls=%async_computation.1 | async-start | bytes 8388608 | tf_op jit(solution)/shard_map/all_to_all | solution.py:13
  24.5 95.1 %copy-start.2 = (bf16[512,896]{1,0:T(8,128)(2,1)S(1)}, bf16[512,896]{1,0:T(8,128)(2,1)}, u32[]{:S(2)}) copy-start(bf16[512,896]{1,0:T(8,128)(2,1)} %param.6) | copy-start | bytes 2752516
  24.5 95.6 %copy-start.3 = (bf16[512,896]{1,0:T(8,128)(2,1)S(1)}, bf16[512,896]{1,0:T(8,128)(2,1)}, u32[]{:S(2)}) copy-start(bf16[512,896]{1,0:T(8,128)(2,1)} %param.7) | copy-start | bytes 2752516
  113.0 167.2 %all-to-all-start = ((bf16[16,896,256]{2,1,0:T(8,128)(2,1)}), bf16[16,896,256]{2,1,0:T(8,128)(2,1)}, u32[]{:S(2)}, u32[]{:S(2)}) async-start(bf16[16,896,256]{2,1,0:T(8,128)(2,1)} %broadcast_select_fusion), calls=%async_computation | async-start | bytes 14680064 | tf_op jit(solution)/shard_map/all_to_all | solution.py:21
  280.1 322.4 %all-to-all-start.2 = ((f32[896,16,256]{2,0,1:T(8,128)}), f32[896,16,256]{2,0,1:T(8,128)}, u32[]{:S(2)}, u32[]{:S(2)}) async-start(f32[896,16,256]{2,0,1:T(8,128)} %fusion.12), calls=%async_computation.2 | async-start | bytes 29360128 | tf_op jit(solution)/shard_map/all_to_all | solution.py:34
  602.5 20.8 %copy-start.1 = (bf16[4,896,256]{2,1,0:T(8,128)(2,1)S(1)}, bf16[4,896,256]{2,1,0:T(8,128)(2,1)}, u32[]{:S(2)}) copy-start(bf16[4,896,256]{2,1,0:T(8,128)(2,1)} %param.8) | copy-start | bytes 5505028
